TPU v7x, 128 devices: a whole 4x4x4 slice. The times are simulated.
128 devices in a mesh: req: 64 (over z, y, x), col: 2 (over core).
Axes of the slice: x: 4, y: 4, z: 4, core: 2. Of those that a mesh axis runs over, the one named last changes fastest.
Arguments:
- tokens: bfloat16 [32768, 1024], P(('req', 'col')), may hold values from -6 to 6
- norm_gain_pair: float32 [2, 1024], replicated, may hold values from 0.5 to 1.5
- query_key_value_weight: bfloat16 [3, 1024, 1024], P(None, None, 'col'), may hold values from -1 to 1
- head_gate_weight: bfloat16 [2, 1024, 8], P(None, None, 'col'), may hold values from -0.1875 to 0.1875
- decay_logit_bias: float32 [8], P('col'), may hold values from -1 to 1024, as said below
- adapter_down_factor: bfloat16 [64, 1024, 16], P('col'), may hold values from -0.1875 to 0.1875
- adapter_up_factor: bfloat16 [64, 16, 1024], P(None, None, 'col'), may hold values from -1.5 to 1.5
- lengths: int32 [64, 2, 3], P('req'), may hold values from 1 to 128, 256 in all within a row
- request_adapter_index: int32 [64, 6], P('req'), may hold values from 0 to 63
- request_cache_index: int32 [64, 6], P('req'), may hold values from 0 to 511
- caches: bfloat16 [256, 8, 128, 128], P('req', 'col'), may hold values from -6 to 6
- head_output_weight: bfloat16 [1024, 1024], P('col'), may hold values from -0.1875 to 0.1875
- feedforward_weight: bfloat16 [3, 1024, 2816], P(None, None, 'col'), may hold values from -0.1875 to 0.1875
Outputs:
- layer_out: bfloat16 [32768, 1024], P(('req', 'col'))
Inputs may be any that keep to these rules, and one draw needn't show every extreme that they name: The 3 lengths of one device sum to 256, and the longest of them is exactly 128. `request_cache_index`: a value of 256 or more means that the request has no cached memory state. `decay_logit_bias`: at most the logarithm of 512.
All inputs are finite; a program needn't handle non-finite values.
Results may differ from a plain program's by a relative error of at most 0.015.
Values may be sent and summed in bfloat16 or wider, within the bound.
No kernel may reach another device: no remote copies, remote signals or barrier semaphores. Data moves between devices by JAX's collectives and lax.ppermute only.
A program may use at most 192 MiB of HBM per device.

v0:
```python
import math
import jax
import jax.numpy as jnp
import numpy as np
from jax import lax
from jax.sharding import Mesh
from jax.sharding import PartitionSpec as P

epsilon = 1e-05
ROWS = ("z", "y", "x", "col")


def rms_scale(values, gain):
    widened = values.astype(jnp.float32)
    factor = lax.rsqrt(jnp.mean(widened * widened, axis=-1, keepdims=True) + epsilon)
    return (widened * factor * gain).astype(jnp.bfloat16)


def swap(value):
    return lax.ppermute(value, "col", perm=[(0, 1), (1, 0)])


def pair_rows(mine, other, col):
    first = jnp.where(col == 0, mine, other)
    second = jnp.where(col == 0, other, mine)
    return jnp.concatenate([first, second], axis=0)


def on_device(
    tokens,
    norm_gain_pair,
    query_key_value_weight,
    head_gate_weight,
    decay_logit_bias,
    adapter_down_factor,
    adapter_up_factor,
    lengths,
    request_adapter_index,
    request_cache_index,
    caches,
    head_output_weight,
    feedforward_weight,
):
    tok_rows, width = tokens.shape
    col = lax.axis_index("col")
    col_count = 2
    group = tok_rows * col_count
    head_cols = query_key_value_weight.shape[2]
    local_heads = head_gate_weight.shape[2]
    head_size = head_cols // local_heads
    group_lengths = lengths[0].reshape(-1)
    scale = 1.0 / math.sqrt(head_size)
    ff_other = swap(feedforward_weight)
    down_other = swap(adapter_down_factor)
    plane = lax.all_gather(caches, ("y", "x"), axis=0, tiled=True)
    per_plane = plane.shape[0]
    line_index = lax.all_gather(request_cache_index[0], "z", axis=0)
    local = line_index - lax.axis_index("z") * per_plane
    valid = (local >= 0) & (local < per_plane)
    picked = plane[jnp.clip(local, 0, per_plane - 1)]
    slots = jnp.where(valid[:, :, None, None, None], picked, jnp.zeros_like(picked))
    states = lax.psum_scatter(slots, "z", scatter_dimension=0, tiled=True)[0]
    normalized_rows = rms_scale(tokens, norm_gain_pair[0])
    gathered = pair_rows(normalized_rows, swap(normalized_rows), col)
    positions = jnp.arange(group, dtype=jnp.int32)
    ends = jnp.cumsum(group_lengths)
    starts = ends - group_lengths
    member = (
        (positions[:, None] >= starts[None, :]) & (positions[:, None] < ends[None, :])
    ).astype(jnp.float32)
    segment = jnp.sum((positions[:, None] >= ends[None, :]).astype(jnp.int32), axis=1)
    projected = jnp.einsum(
        "td,kdc->ktc", gathered, query_key_value_weight, preferred_element_type=jnp.float32
    )
    half_adapters = adapter_down_factor.shape[0]
    mine_numbers = col * half_adapters + jnp.arange(half_adapters, dtype=jnp.int32)
    other_numbers = (1 - col) * half_adapters + jnp.arange(half_adapters, dtype=jnp.int32)
    wanted = request_adapter_index[0][:, None]
    select_mine = (wanted == mine_numbers[None, :]).astype(jnp.bfloat16)
    select_other = (wanted == other_numbers[None, :]).astype(jnp.bfloat16)
    chosen = (
        jnp.einsum(
            "sa,adr->sdr", select_mine, adapter_down_factor, preferred_element_type=jnp.float32
        )
        + jnp.einsum("sa,adr->sdr", select_other, down_other, preferred_element_type=jnp.float32)
    ).astype(jnp.bfloat16)
    per_request = jnp.einsum("td,sdr->tsr", gathered, chosen, preferred_element_type=jnp.float32)
    low_rank_delta = jnp.sum(member[:, :, None] * per_request, axis=1)
    low_rank_delta = low_rank_delta.astype(jnp.bfloat16)
    adapter_onehot = (
        request_adapter_index[0][:, None]
        == jnp.arange(adapter_up_factor.shape[0], dtype=jnp.int32)[None, :]
    ).astype(jnp.bfloat16)
    up_chosen = jnp.einsum(
        "gq,qjl->gjl", adapter_onehot, adapter_up_factor, preferred_element_type=jnp.float32
    ).astype(jnp.bfloat16)
    delta_all = jnp.einsum(
        "tr,src->tsc", low_rank_delta, up_chosen, preferred_element_type=jnp.float32
    )
    delta = jnp.sum(member[:, :, None] * delta_all, axis=1)
    queries = (projected[0] + delta).astype(jnp.bfloat16).reshape(group, local_heads, head_size)
    keys = projected[1].astype(jnp.bfloat16).reshape(group, local_heads, head_size)
    values = projected[2].astype(jnp.bfloat16).reshape(group, local_heads, head_size)
    gate_terms = jnp.einsum(
        "td,kdh->kth", gathered, head_gate_weight, preferred_element_type=jnp.float32
    )
    log_keep = jax.nn.log_sigmoid(gate_terms[0] + decay_logit_bias[None, :])
    mix_gate = jax.nn.sigmoid(gate_terms[1])
    running = jnp.cumsum(log_keep, axis=0)
    before = running - log_keep
    start_hot = (positions[None, :] == starts[:, None]).astype(jnp.float32)
    start_level = jnp.sum(start_hot[:, :, None] * before[None, :, :], axis=1)
    level = running - jnp.sum(member[:, :, None] * start_level[None, :, :], axis=1)
    from_state = jnp.einsum("thi,shij->tshj", queries, states, preferred_element_type=jnp.float32)
    carried = jnp.sum(member[:, :, None, None] * from_state, axis=1) * jnp.exp(level)[:, :, None]
    scores = jnp.einsum("qhd,khd->hqk", queries, keys, preferred_element_type=jnp.float32) * scale
    allowed = (segment[:, None] == segment[None, :]) & (positions[None, :] <= positions[:, None])
    masked = jnp.where(allowed[None], scores, -jnp.inf)
    peak = jnp.max(masked, axis=2, keepdims=True)
    weights = jnp.exp(masked - peak)
    probs = (weights / jnp.sum(weights, axis=2, keepdims=True)).astype(jnp.bfloat16)
    attended = jnp.einsum("hqk,khd->qhd", probs, values, preferred_element_type=jnp.float32)
    gap = jnp.where(allowed[None], running.T[:, :, None] - running.T[:, None, :], -jnp.inf)
    memory_w = (scores * jnp.exp(gap)).astype(jnp.bfloat16)
    recalled = jnp.einsum("hqk,khd->qhd", memory_w, values, preferred_element_type=jnp.float32)
    recalled = recalled + carried
    factor = lax.rsqrt(jnp.mean(recalled * recalled, axis=2, keepdims=True) + epsilon)
    combined = attended + mix_gate[:, :, None] * recalled * factor
    head_out = combined.astype(jnp.bfloat16).reshape(group, head_cols)
    partial = jnp.dot(head_out, head_output_weight, preferred_element_type=jnp.float32)
    own = lax.dynamic_slice_in_dim(partial, col * tok_rows, tok_rows, axis=0)
    sent = lax.dynamic_slice_in_dim(partial, (1 - col) * tok_rows, tok_rows, axis=0)
    attn_proj = own + swap(sent)
    mixed = (tokens.astype(jnp.float32) + attn_proj).astype(jnp.bfloat16)
    normed_two = rms_scale(mixed, norm_gain_pair[1])

    def feed_half(weight):
        gate_up = jnp.einsum(
            "td,kdf->ktf", normed_two, weight[:2], preferred_element_type=jnp.float32
        )
        hidden = (jax.nn.silu(gate_up[0]) * gate_up[1]).astype(jnp.bfloat16)
        return jnp.einsum("tf,df->td", hidden, weight[2], preferred_element_type=jnp.float32)

    feed = feed_half(feedforward_weight) + feed_half(ff_other)
    return (mixed.astype(jnp.float32) + feed).astype(jnp.bfloat16)


def solution(mesh):
    n_req = mesh.shape["req"]
    side = round(n_req ** (1.0 / 3.0))
    devices = np.asarray(mesh.devices).reshape(
        side, side, n_req // (side * side), mesh.shape["col"]
    )
    grid = Mesh(devices, ROWS)
    placed = (
        P(ROWS, None),
        P(),
        P(None, None, "col"),
        P(None, None, "col"),
        P("col"),
        P("col", None, None),
        P(None, None, "col"),
        P(ROWS[:3], None, None),
        P(ROWS[:3], None),
        P(ROWS[:3], None),
        P(ROWS[:3], "col", None, None),
        P("col", None),
        P(None, None, "col"),
    )
    return jax.shard_map(
        on_device, mesh=grid, in_specs=placed, out_specs=P(ROWS, None), check_vma=False
    )
```

profile of v0, /device:TPU:1, one launch (start us, length us, event | category | flops | bytes accessed | tf_op | source)
XLA Modules:
  0.0 177.2 jit_solution(17302642569815768344)
XLA Ops:
  7.3 10.1 %all-gather = s32[4,1,6]{2,1,0:T(1,128)S(1)} all-gather(s32[1,1,6]{2,1,0:T(1,128)} %bitcast.159), channel_id=1, replica_groups=mesh['z'=4,'y'=4,'x'=4,'col'=2] {'z'}, dimensions={0}, use_global_device_ids=true | all-gather | bytes 120 | tf_op jit(solution)/shard_map/all_gather | solution.py:57
  17.5 1.2 fusion.33
  18.7 1.4 fusion.95
  20.1 63.2 %all-gather.3.cloned.1.call-done = bf16[64,4,128,128]{3,2,1,0:T(8,128)(2,1)} async-done(((bf16[4,4,128,128]{3,2,1,0:T(8,128)(2,1)}), bf16[64,4,128,128]{3,2,1,0:T(8,128)(2,1)}) %all-gather.3.cloned.1.call-update) | async-done | bytes 8388624 | tf_op jit(solution)/shard_map/all_gather | solution.py:55
  83.4 6.2 %gather_fusion = bf16[24,4,128,128]{3,2,1,0:T(8,128)(2,1)} fusion(bf16[64,4,128,128]{3,2,1,0:T(8,128)(2,1)} %all-gather.3.cloned.1.call-done, s32[1024]{0:T(1024)S(1)} %pad_clamp_fusion), kind=kCustom, calls=%fused_computation | custom fusion | bytes 6291552 | tf_op jit(solution)/shard_map/gather | solution.py:60
  89.5 4.7 %copy.59 = bf16[4,6,4,128,128]{3,4,1,2,0:T(8,128)(2,1)} copy(bf16[4,6,4,128,128]{4,3,2,1,0:T(8,128)(2,1)} %bitcast.136) | data formatting | bytes 6291456 | tf_op jit(solution)/shard_map/gather | solution.py:60
  94.3 3.8 %broadcast_select_fusion = bf16[4,6,4,128,128]{3,4,1,2,0:T(8,128)(2,1)} fusion(bf16[4,6,4,128,128]{3,4,1,2,0:T(8,128)(2,1)} %copy.59, pred[4,6]{1,0:T(4,128)(4,1)S(1)} %bitcast.156), kind=kLoop, calls=%fused_computation.16 | loop fusion | flops 1572864 | bytes 6291480 | tf_op jit(solution)/shard_map/jit(_where)/select_n | solution.py:61
  98.1 2.0 %fusion.35 = bf16[256,1024]{1,0:T(8,128)(2,1)} fusion(bf16[256,1024]{1,0:T(8,128)(2,1)} %param.13, f32[1024]{0:T(1024)S(1)} %bitcast.146, f32[256]{0:T(256)S(1)} %add_rsqrt_fusion.2), kind=kLoop, calls=%fused_computation.52 | loop fusion | flops 1048576 | bytes 1053696 | tf_op jit(solution)/shard_map/convert_element_type | solution.py:16
  100.9 2.8 %copy.49 = bf16[32,1024,16]{1,0,2:T(8,128)(2,1)} copy(bf16[32,1024,16]{1,2,0:T(8,128)(2,1)} %param.18) | data formatting | bytes 2097152 | tf_op args[5]
  106.5 2.7 %convolution_convert_fusion = bf16[6,16,512]{2,0,1:T(8,128)(2,1)S(1)} fusion(bf16[64,16,512]{2,1,0:T(8,128)(2,1)} %param.19, s32[6]{0:T(128)} %bitcast.151), kind=kOutput, calls=%fused_computation.48 | convolution fusion | flops 6340992 | bytes 1146904 | tf_op jit(solution)/shard_map/gq,qjl->gjl/dot_general | solution.py:94
  109.3 3.2 %fusion.73 = f32[6,1024,16]{1,0,2:T(8,128)} fusion(s32[32]{0:T(128)} %iota_add_fusion.1, s32[6]{0:T(128)} %bitcast.152, bf16[32,1024,16]{1,2,0:T(8,128)(2,1)} %param.18), kind=kOutput, calls=%fused_computation.111 | convolution fusion | flops 6291648 | bytes 1441944 | tf_op jit(solution)/shard_map/sa,adr->sdr/dot_general | solution.py:82
  112.5 1.6 broadcast_select_fusion.2
  114.9 1.1 convolution_bitcast_fusion.1
  117.3 1.3 reshape.277
  118.6 3.0 %reduce-window.18 = f32[4,4,128]{2,1,0:T(4,128)} reduce-window(f32[4,4,128]{2,1,0:T(4,128)} %reshape.277, f32[]{:T(128)} %constant.20.clone.1), window={size=1x1x128 pad=0_0x0_0x127_0}, to_apply=%region_7.8 | reduce-window | flops 260096 | bytes 16388 | tf_op jit(solution)/shard_map/reduce-window.1
  121.6 1.4 slice_reduce_fusion
  123.0 1.3 reduce-window.19
  125.2 3.1 %fusion.96 = (bf16[3,512,512]{1,2,0:T(8,128)(2,1)S(1)}, f32[3,512,512]{1,2,0:T(8,128)S(1)}) fusion(bf16[3,1024,512]{2,1,0:T(8,128)(2,1)S(1)} %copy-done, bf16[256,1024]{1,0:T(8,128)(2,1)} %copy-done.7, bf16[256,1024]{1,0:T(8,128)(2,1)} %copy-done.5), kind=kOutput, calls=%fused_computation.141 | convolution fusion | flops 1613496320 | bytes 8912896 | tf_op jit(solution)/shard_map/td,kdc->ktc/dot_general | solution.py:72
  130.5 1.1 fusion.94
  131.6 1.6 fusion.32
  133.8 1.0 multiply_reduce_fusion
  135.4 4.7 %fusion.97 = (f32[4,512]{1,0:T(4,128)S(1)}, f32[4,512,512]{1,2,0:T(8,128)}) fusion(pred[512,512]{0,1:T(8,128)(4,1)S(1)} %fusion.43, bf16[512,4,128]{0,2,1:T(8,128)(2,1)S(1)} %add_convert_fusion, bf16[512,4,128]{0,2,1:T(8,128)(2,1)} %bitcast.142), kind=kOutput, calls=%fused_computation.142 | convolution fusion | flops 272630272 | bytes 5513216 | tf_op jit(solution)/shard_map/sub | solution.py:120
  140.1 2.2 %fusion.1 = f32[512,4,128]{0,2,1:T(8,128)S(1)} fusion(f32[512,6]{0,1:T(8,128)S(1)} %fusion.60, bf16[1,6,4,128,128]{3,4,1,2,0:T(8,128)(2,1)} %reduce-scatter.2.cloned.1.call-done, bf16[512,4,128]{0,2,1:T(8,128)(2,1)S(1)} %add_convert_fusion), kind=kOutput, calls=%fused_computation.3 | convolution fusion | flops 405536768 | bytes 2371584 | tf_op jit(solution)/shard_map/thi,shij->tshj/dot_general | solution.py:114
  142.4 2.9 %multiply_reduce_fusion.1 = (f32[512,4]{0,1:T(4,128)S(1)}, f32[512,4,128]{0,2,1:T(8,128)}) fusion(f32[512,4,128]{0,2,1:T(8,128)S(1)} %fusion.1, f32[512,4]{0,1:T(4,128)S(1)} %copy-done.16, bf16[512,4,128]{0,2,1:T(8,128)(2,1)S(1)} %bitcast.140, f32[4,512]{1,0:T(4,128)S(1)} %bitcast.149, pred[512,512]{0,1:T(8,128)(4,1)S(1)} %fusion.43, ...), kind=kOutput, calls=%fused_computation.61 | convolution fusion | flops 543160320 | bytes 3956736 | tf_op jit(solution)/shard_map/hqk,khd->qhd/dot_general | solution.py:125
  145.3 3.1 %fusion.30 = bf16[512,4,128]{0,2,1:T(8,128)(2,1)S(1)} fusion(bf16[512,4,128]{0,2,1:T(8,128)(2,1)S(1)} %bitcast.141, f32[4,512,512]{1,2,0:T(8,128)} %get-tuple-element.16, f32[4,512]{1,0:T(4,128)S(1)} %get-tuple-element.15, f32[512,4,128]{0,2,1:T(8,128)} %get-tuple-element.18, f32[512,4]{0,1:T(4,128)S(1)} %add_rsqrt_fusion, f32[512,4]{0,1:T(4,128)S(1)} %copy-done.17), kind=kOutput, calls=%fused_computation.44 | convolution fusion | flops 271581184 | bytes 6316032 | tf_op jit(solution)/shard_map/hqk,khd->qhd/dot_general | solution.py:122
  149.2 1.2 constant_dynamic-slice_fusion
  150.4 3.0 %collective-permute-done.2 = f32[256,1024]{1,0:T(8,128)} collective-permute-done((f32[256,1024]{1,0:T(8,128)}, f32[256,1024]{1,0:T(8,128)}, u32[]{:S(2)}, u32[]{:S(2)}) %collective-permute-start.2) | collective-permute-done | bytes 1048608 | tf_op jit(solution)/shard_map/ppermute | solution.py:20
  153.4 1.5 fusion.37
  154.9 4.4 %fusion.6 = f32[2,256,1408]{2,1,0:T(8,128)S(1)} fusion(bf16[3,1024,1408]{2,1,0:T(8,128)(2,1)} %param.25, bf16[256,1024]{1,0:T(8,128)(2,1)S(1)} %get-tuple-element.6, f32[1024]{0:T(1024)S(1)} %bitcast.154, f32[256]{0:T(256)S(1)} %add_rsqrt_fusion.1), kind=kOutput, calls=%fused_computation.13 | convolution fusion | flops 1477443584 | bytes 9180160 | tf_op jit(solution)/shard_map/td,kdf->ktf/dot_general | solution.py:138
  159.3 2.9 %fusion.14 = f32[256,1024]{1,0:T(8,128)S(1)} fusion(bf16[3,1024,1408]{2,1,0:T(8,128)(2,1)} %param.25, f32[2,256,1408]{2,1,0:T(8,128)S(1)} %fusion.6), kind=kOutput, calls=%fused_computation.19 | convolution fusion | flops 740360192 | bytes 6815744 | tf_op jit(solution)/shard_map/tf,df->td/dot_general | solution.py:142
  162.2 4.4 %fusion.9 = f32[2,256,1408]{2,1,0:T(8,128)S(1)} fusion(bf16[3,1024,1408]{2,1,0:T(8,128)(2,1)} %collective-permute-done.3, bf16[256,1024]{1,0:T(8,128)(2,1)S(1)} %get-tuple-element.6, f32[1024]{0:T(1024)S(1)} %bitcast.155, f32[256]{0:T(256)S(1)} %add_rsqrt_fusion.1), kind=kOutput, calls=%fused_computation.14 | convolution fusion | flops 1477443584 | bytes 9180160 | tf_op jit(solution)/shard_map/td,kdf->ktf/dot_general | solution.py:138
  166.5 3.8 %fusion.31 = bf16[256,1024]{1,0:T(8,128)(2,1)} fusion(f32[256,1024]{1,0:T(8,128)S(1)} %fusion.14, bf16[3,1024,1408]{2,1,0:T(8,128)(2,1)} %collective-permute-done.3, bf16[256,1024]{1,0:T(8,128)(2,1)S(1)} %get-tuple-element.6, f32[2,256,1408]{2,1,0:T(8,128)S(1)} %fusion.9), kind=kOutput, calls=%fused_computation.45 | convolution fusion | flops 741408768 | bytes 7864320 | tf_op jit(solution)/shard_map/tf,df->td/dot_general | solution.py:142
  (96 shorter events, 11.5 us)
Async XLA Ops:
  6.5 118.6 %copy-start = (bf16[3,1024,512]{2,1,0:T(8,128)(2,1)S(1)}, bf16[3,1024,512]{2,1,0:T(8,128)(2,1)}, u32[]{:S(2)}) copy-start(bf16[3,1024,512]{2,1,0:T(8,128)(2,1)} %param.15) | copy-start | bytes 9437188
  6.5 76.8 %all-gather.3.cloned.1.call-start = ((), (), s32[]{:S(2)}) async-start(), calls=%async_computation.1 | async-start | bytes 8912896 | tf_op jit(solution)/shard_map/all_gather | solution.py:55
  7.3 132.8 %reduce-scatter.2.cloned.1.call-start = ((), (), s32[]{:S(2)}) async-start(), calls=%async_computation.2 | async-start | bytes 3932160 | tf_op jit(solution)/shard_map/reduce_scatter | solution.py:62
  20.1 78.0 %copy-start.12 = (f32[1,1024]{1,0:T(1,128)}, f32[1,1024]{1,0:T(1,128)S(1)}, u32[]{:S(2)}) copy-start(f32[1,1024]{1,0:T(1,128)S(1)} %get-tuple-element.12) | copy-start | bytes 12292
  98.1 6.0 %copy-start.24 = (s32[1,2,3]{2,1,0:T(2,128)S(1)}, s32[1,2,3]{2,1,0:T(2,128)}, u32[]{:S(2)}) copy-start(s32[1,2,3]{2,1,0:T(2,128)} %param.20) | copy-start | bytes 76
  98.1 2.0 %copy-start.15 = (f32[256]{0:T(256)}, f32[256]{0:T(256)S(1)}, u32[]{:S(2)}) copy-start(f32[256]{0:T(256)S(1)} %add_rsqrt_fusion.2) | copy-start | bytes 3076
  100.2 12.4 %collective-permute-start = (bf16[256,1024]{1,0:T(8,128)(2,1)}, bf16[256,1024]{1,0:T(8,128)(2,1)}, u32[]{:S(2)}, u32[]{:S(2)}) collective-permute-start(bf16[256,1024]{1,0:T(8,128)(2,1)} %fusion.35), channel_id=1, source_target_pairs={{0,1},{1,0},{2,3},{3,2},{4,5},{5,4},{6,7},{7,6},{8,9},{9,8},{10,11... | collective-permute-start | bytes 1572872 | tf_op jit(solution)/shard_map/ppermute | solution.py:20
  103.6 27.9 %collective-permute-start.1 = (bf16[32,1024,16]{1,0,2:T(8,128)(2,1)}, bf16[32,1024,16]{1,0,2:T(8,128)(2,1)}, u32[]{:S(2)}, u32[]{:S(2)}) collective-permute-start(bf16[32,1024,16]{1,0,2:T(8,128)(2,1)} %copy.49), channel_id=1, source_target_pairs={{0,1},{1,0},{2,3},{3,2},{4,5},{5,4},{6,7},{7,6},{8,9},{9,8},{10,11... | collective-permute-start | bytes 3145736 | tf_op jit(solution)/shard_map/ppermute | solution.py:20
  103.6 58.5 %collective-permute-start.3 = (bf16[3,1024,1408]{2,1,0:T(8,128)(2,1)}, bf16[3,1024,1408]{2,1,0:T(8,128)(2,1)}, u32[]{:S(2)}, u32[]{:S(2)}) collective-permute-start(bf16[3,1024,1408]{2,1,0:T(8,128)(2,1)} %param.25), channel_id=1, source_target_pairs={{0,1},{1,0},{2,3},{3,2},{4,5},{5,4},{6,7},{7,6},{8,9},{9,8},{10,11... | collective-permute-start | bytes 25952264 | tf_op jit(solution)/shard_map/ppermute | solution.py:20
  106.5 10.1 %copy-start.21 = (f32[4]{0:T(128)S(1)}, f32[4]{0:T(128)}, u32[]{:S(2)}) copy-start(f32[4]{0:T(128)} %param.17) | copy-start | bytes 52
  114.1 0.8 copy-start.5
  114.1 1.9 %copy-start.7 = (bf16[256,1024]{1,0:T(8,128)(2,1)}, bf16[256,1024]{1,0:T(8,128)(2,1)S(1)}, u32[]{:S(2)}) copy-start(bf16[256,1024]{1,0:T(8,128)(2,1)S(1)} %get-tuple-element.10) | copy-start | bytes 1572868
  116.0 0.6 copy-start.13
  125.1 3.1 %copy-start.14 = (f32[2,512,4]{1,2,0:T(4,128)S(1)}, f32[2,512,4]{1,2,0:T(4,128)}, u32[]{:S(2)}) copy-start(f32[2,512,4]{1,2,0:T(4,128)} %copy-done.13) | copy-start | bytes 49156
  125.1 3.1 %copy-start.22 = (f32[4]{0:T(128)S(1)}, f32[4]{0:T(128)}, u32[]{:S(2)}) copy-start(f32[4]{0:T(128)} %param.17) | copy-start | bytes 52
  125.1 3.9 %copy-start.11 = (f32[6,512]{1,0:T(8,128)S(1)}, f32[6,512]{1,0:T(8,128)}, u32[]{:S(2)}) copy-start(f32[6,512]{1,0:T(8,128)} %fusion.61) | copy-start | bytes 36868
  128.3 3.3 %copy-start.3 = (f32[6,1024,16]{1,0,2:T(8,128)S(1)}, f32[6,1024,16]{1,0,2:T(8,128)}, u32[]{:S(2)}) copy-start(f32[6,1024,16]{1,0,2:T(8,128)} %fusion.73) | copy-start | bytes 1179652
  128.3 3.3 %copy-start.19 = (s32[1,6]{1,0:T(1,128)S(1)}, s32[1,6]{1,0:T(1,128)}, u32[]{:S(2)}) copy-start(s32[1,6]{1,0:T(1,128)} %param.21) | copy-start | bytes 76
  128.3 3.3 %copy-start.23 = (s32[32]{0:T(128)S(1)}, s32[32]{0:T(128)}, u32[]{:S(2)}) copy-start(s32[32]{0:T(128)} %iota_add_fusion) | copy-start | bytes 388
  129.0 4.3 %copy-start.6 = (bf16[256,1024]{1,0:T(8,128)(2,1)S(1)}, bf16[256,1024]{1,0:T(8,128)(2,1)}, u32[]{:S(2)}) copy-start(bf16[256,1024]{1,0:T(8,128)(2,1)} %copy-done.5) | copy-start | bytes 1572868
  129.0 4.3 %copy-start.8 = (bf16[256,1024]{1,0:T(8,128)(2,1)S(1)}, bf16[256,1024]{1,0:T(8,128)(2,1)}, u32[]{:S(2)}) copy-start(bf16[256,1024]{1,0:T(8,128)(2,1)} %copy-done.7) | copy-start | bytes 1572868
  140.1 2.3 %copy-start.9 = (bf16[1,512,512]{1,2,0:T(8,128)(2,1)S(1)}, bf16[1,512,512]{1,2,0:T(8,128)(2,1)}, u32[]{:S(2)}) copy-start(bf16[1,512,512]{1,2,0:T(8,128)(2,1)} %get-tuple-element.8) | copy-start | bytes 1572868
  140.1 2.3 %copy-start.10 = (bf16[1,512,512]{1,2,0:T(8,128)(2,1)S(1)}, bf16[1,512,512]{1,2,0:T(8,128)(2,1)}, u32[]{:S(2)}) copy-start(bf16[1,512,512]{1,2,0:T(8,128)(2,1)} %get-tuple-element.7) | copy-start | bytes 1572868
  140.1 2.3 %copy-start.16 = (f32[512,4]{0,1:T(4,128)S(1)}, f32[512,4]{0,1:T(4,128)}, u32[]{:S(2)}) copy-start(f32[512,4]{0,1:T(4,128)} %fusion.69) | copy-start | bytes 24580
  140.1 2.3 %copy-start.18 = (f32[1,4,4,128]{3,1,2,0:T(4,128)S(1)}, f32[1,4,4,128]{3,1,2,0:T(4,128)}, u32[]{:S(2)}) copy-start(f32[1,4,4,128]{3,1,2,0:T(4,128)} %copy.83) | copy-start | bytes 24580
  142.4 2.9 %copy-start.17 = (f32[512,4]{0,1:T(4,128)S(1)}, f32[512,4]{0,1:T(4,128)}, u32[]{:S(2)}) copy-start(f32[512,4]{0,1:T(4,128)} %fusion.68) | copy-start | bytes 24580
  145.3 3.1 %copy-start.4 = (bf16[512,1024]{1,0:T(8,128)(2,1)S(1)}, bf16[512,1024]{1,0:T(8,128)(2,1)}, u32[]{:S(2)}) copy-start(bf16[512,1024]{1,0:T(8,128)(2,1)} %param.24) | copy-start | bytes 3145732
  148.4 5.0 %copy-start.2 = (bf16[256,1024]{1,0:T(8,128)(2,1)S(1)}, bf16[256,1024]{1,0:T(8,128)(2,1)}, u32[]{:S(2)}) copy-start(bf16[256,1024]{1,0:T(8,128)(2,1)} %param.13) | copy-start | bytes 1572868
  149.2 5.7 %copy-start.20 = (f32[1,1024]{1,0:T(1,128)S(1)}, f32[1,1024]{1,0:T(1,128)}, u32[]{:S(2)}) copy-start(f32[1,1024]{1,0:T(1,128)} %get-tuple-element.11) | copy-start | bytes 12292
  150.4 3.0 %collective-permute-start.2 = (f32[256,1024]{1,0:T(8,128)}, f32[256,1024]{1,0:T(8,128)}, u32[]{:S(2)}, u32[]{:S(2)}) collective-permute-start(f32[256,1024]{1,0:T(8,128)} %constant_dynamic-slice_fusion), channel_id=1, source_target_pairs={{0,1},{1,0},{2,3},{3,2},{4,5},{5,4},{6,7},{7,6},{8,9},{9,8},{10,11... | collective-permute-start | bytes 3145736 | tf_op jit(solution)/shard_map/ppermute | solution.py:20
  166.5 3.9 %copy-start.1 = (bf16[3,1024,512]{2,1,0:T(8,128)(2,1)S(1)}, bf16[3,1024,512]{2,1,0:T(8,128)(2,1)}, u32[]{:S(2)}) copy-start(bf16[3,1024,512]{2,1,0:T(8,128)(2,1)} %param.15) | copy-start | bytes 9437188
Sparse Core Ops, SparseCore 0:
  9.5 73.8 all-gather.2
  98.2 38.2 reduce-scatter.1
where the time goes:
time: 178 us; the launch traced here: 177 us
  waiting for transfers between devices  67 us (38%)
  matrix products  42.3 us (24%)
  local copies, waits for them, and re-layouts  22.9 us (13%)
  other arithmetic  20 us (11%)
  between operations  13.8 us (8%)
  blocking collectives  10.1 us (6%)
    all_gather x1, waiting for transfers between devices, on_device(): plane = lax.all_gather(caches, ('y', 'x'), axis=0, tiled=True)  63.2 us
    gather x2, local copies, waits for them, and re-layouts, on_device(): picked = plane[jnp.clip(local, 0, per_plane - 1)]  10.9 us
    all_gather x1, blocking collectives, on_device(): line_index = lax.all_gather(request_cache_index[0], 'z', axis=0)  10.1 us
    dot_general x2, matrix products, feed_half(): jnp.einsum('td,kdf->ktf', normed_two, weight[:2], preferred_element_type=...  8.73 us
    dot_general x2, matrix products, feed_half(): jnp.einsum('tf,df->td', hidden, weight[2], preferred_element_type=jnp.flo...  6.71 us
    unnamed x53, local copies, waits for them, and re-layouts  4.86 us
    sub x1, matrix products, on_device(): weights = jnp.exp(masked - peak)  4.67 us
    another operation x3, other arithmetic  4.54 us
  transfers between devices with their start and end apart: 6, of which 2 were waited for; matrix products, arithmetic and copies ran while one was open for 34% of the time, Pallas kernels for 0%

commit v1 on v0

--- a/solution.py
+++ b/solution.py
@@ -1,3 +1,4 @@
+import functools
 import math
 import jax
 import jax.numpy as jnp
@@ -8,6 +9,15 @@
 
 epsilon = 1e-05
 ROWS = ("z", "y", "x", "col")
+
+
+def fill_task(v0, mesh_ax):
+    r_now = jnp.stack([v0 for _ in range(lax.psum(1, mesh_ax))], axis=0)
+    ready = lax.all_to_all(r_now, mesh_ax, 0, 0)
+    return jnp.concatenate(ready, 0)
+
+
+choose_cubes = functools.partial(fill_task, mesh_ax=("y", "x"))
 
 
 def rms_scale(values, gain):
@@ -52,7 +62,7 @@
     scale = 1.0 / math.sqrt(head_size)
     ff_other = swap(feedforward_weight)
     down_other = swap(adapter_down_factor)
-    plane = lax.all_gather(caches, ("y", "x"), axis=0, tiled=True)
+    plane = choose_cubes(caches)
     per_plane = plane.shape[0]
     line_index = lax.all_gather(request_cache_index[0], "z", axis=0)
     local = line_index - lax.axis_index("z") * per_plane

time: 178 us -> 235 us (1.32)
  waiting for transfers between devices: 67 us -> 115 us
  starting transfers between devices: 1.23 us -> 10.2 us
    all_to_all x0 -> x1, waiting for transfers between devices: none -> 112 us  [fill_task(): ready = lax.all_to_all(r_now, mesh_ax, 0, 0)]
    all_gather x1 -> x0, waiting for transfers between devices: 63.2 us -> none  [on_device(): plane = lax.all_gather(caches, ('y', 'x'), axis=0, tiled=True)]
    all_to_all x0 -> x1, starting transfers between devices: none -> 7.77 us  [fill_task(): ready = lax.all_to_all(r_now, mesh_ax, 0, 0)]
    another operation x2 -> x3, local copies, waits for them, and re-layouts: 1.39 us -> 7.92 us  [the longest x1 6.54 us: fill_task(): r_now = jnp.stack([v0 for _ in range(lax.psum(1, mesh_ax))], axis=0)]
    gather x2 -> x1, local copies, waits for them, and re-layouts: 10.9 us -> 6.19 us  [on_device(): picked = plane[jnp.clip(local, 0, per_plane - 1)]]
    unnamed x53 -> x57, local copies, waits for them, and re-layouts: 4.86 us -> 4.87 us
  transfers between devices with their start and end apart: 6 -> 6, of which waited for: 2 -> 2; matrix products, arithmetic and copies ran while one was open for 34% -> 25% of each run, Pallas kernels for 0% -> 0%
where the time goes in v1:
time: 235 us; the launch traced here: 234 us
  waiting for transfers between devices  115 us (49%)
  matrix products  42 us (18%)
  local copies, waits for them, and re-layouts  23.9 us (10%)
  other arithmetic  20 us (9%)
  between operations  13.8 us (6%)
  starting transfers between devices  10.2 us (4%)
  blocking collectives  9.33 us (4%)
    all_to_all x1, waiting for transfers between devices, fill_task(): ready = lax.all_to_all(r_now, mesh_ax, 0, 0)  112 us
    all_gather x1, blocking collectives, on_device(): line_index = lax.all_gather(request_cache_index[0], 'z', axis=0)  9.33 us
    dot_general x2, matrix products, feed_half(): jnp.einsum('td,kdf->ktf', normed_two, weight[:2], preferred_element_type=...  8.73 us
    all_to_all x1, starting transfers between devices, fill_task(): ready = lax.all_to_all(r_now, mesh_ax, 0, 0)  7.77 us
    dot_general x2, matrix products, feed_half(): jnp.einsum('tf,df->td', hidden, weight[2], preferred_element_type=jnp.flo...  6.71 us
    another operation x1, local copies, waits for them, and re-layouts, fill_task(): r_now = jnp.stack([v0 for _ in range(lax.psum(1, mesh_ax))], axis=0)  6.54 us
    gather x1, local copies, waits for them, and re-layouts, on_device(): picked = plane[jnp.clip(local, 0, per_plane - 1)]  6.19 us
    unnamed x57, local copies, waits for them, and re-layouts  4.87 us
  transfers between devices with their start and end apart: 6, of which 2 were waited for; matrix products, arithmetic and copies ran while one was open for 25% of the time, Pallas kernels for 0%

profile of v1, /device:TPU:1, one launch (start us, length us, event | category | flops | bytes accessed | tf_op | source)
XLA Modules:
  0.0 234.0 jit_solution(13461446147499477883)
XLA Ops:
  6.5 6.5 %stack.2 = bf16[16,4,4,128,128]{4,3,2,1,0:T(8,128)(2,1)} broadcast(bf16[4,4,128,128]{3,2,1,0:T(8,128)(2,1)} %param.23), dimensions={1,2,3,4} | broadcast | bytes 8912896 | tf_op jit(solution)/shard_map/stack | solution.py:15
  13.1 7.8 %all-to-all-start = ((bf16[16,4,4,128,128]{4,3,2,1,0:T(8,128)(2,1)}), bf16[16,4,4,128,128]{4,3,2,1,0:T(8,128)(2,1)}, u32[]{:S(2)}, u32[]{:S(2)}) async-start(bf16[16,4,4,128,128]{4,3,2,1,0:T(8,128)(2,1)} %stack.2), calls=%async_computation | async-start | bytes 16777216 | tf_op jit(solution)/shard_map/all_to_all | solution.py:16
  20.9 9.3 %all-gather = s32[4,1,6]{2,1,0:T(1,128)S(1)} all-gather(s32[1,1,6]{2,1,0:T(1,128)S(1)} %bitcast.161), channel_id=1, replica_groups=mesh['z'=4,'y'=4,'x'=4,'col'=2] {'z'}, dimensions={0}, use_global_device_ids=true | all-gather | bytes 120 | tf_op jit(solution)/shard_map/all_gather | solution.py:67
  30.4 1.2 fusion.33
  32.2 111.8 %all-to-all-done = bf16[16,4,4,128,128]{4,3,2,1,0:T(8,128)(2,1)} async-done(((bf16[16,4,4,128,128]{4,3,2,1,0:T(8,128)(2,1)}), bf16[16,4,4,128,128]{4,3,2,1,0:T(8,128)(2,1)}, u32[]{:S(2)}, u32[]{:S(2)}) %all-to-all-start) | async-done | bytes 8388640 | tf_op jit(solution)/shard_map/all_to_all | solution.py:16
  144.0 6.2 %gather_fusion = bf16[24,4,128,128]{3,2,1,0:T(8,128)(2,1)} fusion(bf16[64,4,128,128]{3,2,1,0:T(8,128)(2,1)} %bitcast.23, s32[1024]{0:T(1024)S(1)} %pad_clamp_fusion), kind=kCustom, calls=%fused_computation | custom fusion | bytes 6291552 | tf_op jit(solution)/shard_map/gather | solution.py:70
  150.2 3.8 %broadcast_select_fusion = bf16[4,6,4,128,128]{4,3,2,1,0:T(8,128)(2,1)} fusion(bf16[4,6,4,128,128]{4,3,2,1,0:T(8,128)(2,1)} %bitcast.138, pred[4,6]{1,0:T(4,128)(4,1)S(1)} %bitcast.158), kind=kLoop, calls=%fused_computation.16 | loop fusion | flops 1572864 | bytes 6291480 | tf_op jit(solution)/shard_map/jit(_where)/select_n | solution.py:71
  154.0 2.0 fusion.35
  156.1 1.8 collective-permute-start
  157.9 2.8 %copy.48 = bf16[32,1024,16]{1,0,2:T(8,128)(2,1)} copy(bf16[32,1024,16]{1,2,0:T(8,128)(2,1)} %param.18) | data formatting | bytes 2097152 | tf_op args[5]
  163.6 2.5 %convolution_convert_fusion = bf16[6,16,512]{2,0,1:T(8,128)(2,1)S(1)} fusion(bf16[64,16,512]{2,1,0:T(8,128)(2,1)} %param.19, s32[6]{0:T(128)} %bitcast.153), kind=kOutput, calls=%fused_computation.48 | convolution fusion | flops 6340992 | bytes 1146904 | tf_op jit(solution)/shard_map/gq,qjl->gjl/dot_general | solution.py:104
  166.1 3.2 %fusion.73 = f32[6,1024,16]{1,0,2:T(8,128)} fusion(s32[32]{0:T(128)} %iota_add_fusion.1, s32[6]{0:T(128)} %bitcast.154, bf16[32,1024,16]{1,2,0:T(8,128)(2,1)} %param.18), kind=kOutput, calls=%fused_computation.111 | convolution fusion | flops 6291648 | bytes 1441944 | tf_op jit(solution)/shard_map/sa,adr->sdr/dot_general | solution.py:92
  169.3 1.5 broadcast_select_fusion.2
  171.7 1.1 convolution_bitcast_fusion.1
  174.1 1.3 reshape.282
  175.4 3.0 %reduce-window.18 = f32[4,4,128]{2,1,0:T(4,128)} reduce-window(f32[4,4,128]{2,1,0:T(4,128)} %reshape.282, f32[]{:T(128)} %constant.20.clone.1), window={size=1x1x128 pad=0_0x0_0x127_0}, to_apply=%region_7.8 | reduce-window | flops 260096 | bytes 16388 | tf_op jit(solution)/shard_map/reduce-window.1
  178.4 1.4 slice_reduce_fusion
  179.8 1.3 reduce-window.19
  181.9 3.1 %fusion.96 = (bf16[3,512,512]{1,2,0:T(8,128)(2,1)S(1)}, f32[3,512,512]{1,2,0:T(8,128)S(1)}) fusion(bf16[3,1024,512]{2,1,0:T(8,128)(2,1)S(1)} %copy-done, bf16[256,1024]{1,0:T(8,128)(2,1)} %copy-done.7, bf16[256,1024]{1,0:T(8,128)(2,1)} %copy-done.5), kind=kOutput, calls=%fused_computation.141 | convolution fusion | flops 1613496320 | bytes 8912896 | tf_op jit(solution)/shard_map/td,kdc->ktc/dot_general | solution.py:82
  187.2 1.1 fusion.94
  188.3 1.6 fusion.32
  192.1 4.7 %fusion.97 = (f32[4,512]{1,0:T(4,128)S(1)}, f32[4,512,512]{1,2,0:T(8,128)}) fusion(pred[512,512]{0,1:T(8,128)(4,1)S(1)} %fusion.43, bf16[512,4,128]{0,2,1:T(8,128)(2,1)S(1)} %add_convert_fusion, bf16[512,4,128]{0,2,1:T(8,128)(2,1)} %bitcast.144), kind=kOutput, calls=%fused_computation.142 | convolution fusion | flops 272630272 | bytes 5513216 | tf_op jit(solution)/shard_map/sub | solution.py:130
  196.9 2.3 fusion.1
  199.2 2.9 %multiply_reduce_fusion.1 = (f32[512,4]{0,1:T(4,128)S(1)}, f32[512,4,128]{0,2,1:T(8,128)}) fusion(f32[512,4,128]{0,2,1:T(8,128)S(1)} %fusion.1, f32[512,4]{0,1:T(4,128)S(1)} %copy-done.16, bf16[512,4,128]{0,2,1:T(8,128)(2,1)S(1)} %bitcast.142, f32[4,512]{1,0:T(4,128)S(1)} %bitcast.151, pred[512,512]{0,1:T(8,128)(4,1)S(1)} %fusion.43, ...), kind=kOutput, calls=%fused_computation.61 | convolution fusion | flops 543160320 | bytes 3956736 | tf_op jit(solution)/shard_map/hqk,khd->qhd/dot_general | solution.py:135
  202.1 3.1 %fusion.30 = bf16[512,4,128]{0,2,1:T(8,128)(2,1)S(1)} fusion(bf16[512,4,128]{0,2,1:T(8,128)(2,1)S(1)} %bitcast.143, f32[4,512,512]{1,2,0:T(8,128)} %get-tuple-element.16, f32[4,512]{1,0:T(4,128)S(1)} %get-tuple-element.15, f32[512,4,128]{0,2,1:T(8,128)} %get-tuple-element.18, f32[512,4]{0,1:T(4,128)S(1)} %add_rsqrt_fusion, f32[512,4]{0,1:T(4,128)S(1)} %copy-done.18), kind=kOutput, calls=%fused_computation.44 | convolution fusion | flops 271581184 | bytes 6316032 | tf_op jit(solution)/shard_map/hqk,khd->qhd/dot_general | solution.py:132
  206.0 1.2 constant_dynamic-slice_fusion
  207.2 3.0 %collective-permute-done.2 = f32[256,1024]{1,0:T(8,128)} collective-permute-done((f32[256,1024]{1,0:T(8,128)}, f32[256,1024]{1,0:T(8,128)}, u32[]{:S(2)}, u32[]{:S(2)}) %collective-permute-start.2) | collective-permute-done | bytes 1048608 | tf_op jit(solution)/shard_map/ppermute | solution.py:30
  210.2 1.5 fusion.37
  211.7 4.4 %fusion.6 = f32[2,256,1408]{2,1,0:T(8,128)S(1)} fusion(bf16[3,1024,1408]{2,1,0:T(8,128)(2,1)} %param.25, bf16[256,1024]{1,0:T(8,128)(2,1)S(1)} %get-tuple-element.6, f32[1024]{0:T(1024)S(1)} %bitcast.156, f32[256]{0:T(256)S(1)} %add_rsqrt_fusion.1), kind=kOutput, calls=%fused_computation.13 | convolution fusion | flops 1477443584 | bytes 9180160 | tf_op jit(solution)/shard_map/td,kdf->ktf/dot_general | solution.py:148
  216.1 2.9 %fusion.14 = f32[256,1024]{1,0:T(8,128)S(1)} fusion(bf16[3,1024,1408]{2,1,0:T(8,128)(2,1)} %param.25, f32[2,256,1408]{2,1,0:T(8,128)S(1)} %fusion.6), kind=kOutput, calls=%fused_computation.19 | convolution fusion | flops 740360192 | bytes 6815744 | tf_op jit(solution)/shard_map/tf,df->td/dot_general | solution.py:152
  219.0 4.4 %fusion.9 = f32[2,256,1408]{2,1,0:T(8,128)S(1)} fusion(bf16[3,1024,1408]{2,1,0:T(8,128)(2,1)} %collective-permute-done.3, bf16[256,1024]{1,0:T(8,128)(2,1)S(1)} %get-tuple-element.6, f32[1024]{0:T(1024)S(1)} %bitcast.157, f32[256]{0:T(256)S(1)} %add_rsqrt_fusion.1), kind=kOutput, calls=%fused_computation.14 | convolution fusion | flops 1477443584 | bytes 9180160 | tf_op jit(solution)/shard_map/td,kdf->ktf/dot_general | solution.py:148
  223.4 3.8 %fusion.31 = bf16[256,1024]{1,0:T(8,128)(2,1)} fusion(f32[256,1024]{1,0:T(8,128)S(1)} %fusion.14, bf16[3,1024,1408]{2,1,0:T(8,128)(2,1)} %collective-permute-done.3, bf16[256,1024]{1,0:T(8,128)(2,1)S(1)} %get-tuple-element.6, f32[2,256,1408]{2,1,0:T(8,128)S(1)} %fusion.9), kind=kOutput, calls=%fused_computation.45 | convolution fusion | flops 741408768 | bytes 7864320 | tf_op jit(solution)/shard_map/tf,df->td/dot_general | solution.py:152
  (99 shorter events, 11.8 us)
Async XLA Ops:
  6.5 175.4 %copy-start = (bf16[3,1024,512]{2,1,0:T(8,128)(2,1)S(1)}, bf16[3,1024,512]{2,1,0:T(8,128)(2,1)}, u32[]{:S(2)}) copy-start(bf16[3,1024,512]{2,1,0:T(8,128)(2,1)} %param.15) | copy-start | bytes 9437188
  13.1 7.8 %copy-start.25 = (s32[1,6]{1,0:T(1,128)S(1)}, s32[1,6]{1,0:T(1,128)}, u32[]{:S(2)}) copy-start(s32[1,6]{1,0:T(1,128)} %param.22) | copy-start | bytes 76
  13.1 18.5 %copy-start.17 = (f32[2,1024]{1,0:T(2,128)S(1)}, f32[2,1024]{1,0:T(2,128)}, u32[]{:S(2)}) copy-start(f32[2,1024]{1,0:T(2,128)} %param.14) | copy-start | bytes 24580
  13.1 130.9 %all-to-all-start = ((bf16[16,4,4,128,128]{4,3,2,1,0:T(8,128)(2,1)}), bf16[16,4,4,128,128]{4,3,2,1,0:T(8,128)(2,1)}, u32[]{:S(2)}, u32[]{:S(2)}) async-start(bf16[16,4,4,128,128]{4,3,2,1,0:T(8,128)(2,1)} %stack.2), calls=%async_computation | async-start | bytes 16777216 | tf_op jit(solution)/shard_map/all_to_all | solution.py:16
  20.9 176.0 %reduce-scatter.2.cloned.1.call-start = ((), (), s32[]{:S(2)}) async-start(), calls=%async_computation.2 | async-start | bytes 3932160 | tf_op jit(solution)/shard_map/reduce_scatter | solution.py:72
  32.2 121.8 %copy-start.12 = (f32[1,1024]{1,0:T(1,128)}, f32[1,1024]{1,0:T(1,128)S(1)}, u32[]{:S(2)}) copy-start(f32[1,1024]{1,0:T(1,128)S(1)} %get-tuple-element.12) | copy-start | bytes 12292
  154.0 7.2 %copy-start.26 = (s32[1,2,3]{2,1,0:T(2,128)S(1)}, s32[1,2,3]{2,1,0:T(2,128)}, u32[]{:S(2)}) copy-start(s32[1,2,3]{2,1,0:T(2,128)} %param.20) | copy-start | bytes 76
  154.0 2.0 copy-start.15
  156.1 13.3 %collective-permute-start = (bf16[256,1024]{1,0:T(8,128)(2,1)}, bf16[256,1024]{1,0:T(8,128)(2,1)}, u32[]{:S(2)}, u32[]{:S(2)}) collective-permute-start(bf16[256,1024]{1,0:T(8,128)(2,1)} %fusion.35), channel_id=1, source_target_pairs={{0,1},{1,0},{2,3},{3,2},{4,5},{5,4},{6,7},{7,6},{8,9},{9,8},{10,11... | collective-permute-start | bytes 1572872 | tf_op jit(solution)/shard_map/ppermute | solution.py:30
  160.7 27.6 %collective-permute-start.1 = (bf16[32,1024,16]{1,0,2:T(8,128)(2,1)}, bf16[32,1024,16]{1,0,2:T(8,128)(2,1)}, u32[]{:S(2)}, u32[]{:S(2)}) collective-permute-start(bf16[32,1024,16]{1,0,2:T(8,128)(2,1)} %copy.48), channel_id=1, source_target_pairs={{0,1},{1,0},{2,3},{3,2},{4,5},{5,4},{6,7},{7,6},{8,9},{9,8},{10,11... | collective-permute-start | bytes 3145736 | tf_op jit(solution)/shard_map/ppermute | solution.py:30
  160.7 58.3 %collective-permute-start.3 = (bf16[3,1024,1408]{2,1,0:T(8,128)(2,1)}, bf16[3,1024,1408]{2,1,0:T(8,128)(2,1)}, u32[]{:S(2)}, u32[]{:S(2)}) collective-permute-start(bf16[3,1024,1408]{2,1,0:T(8,128)(2,1)} %param.25), channel_id=1, source_target_pairs={{0,1},{1,0},{2,3},{3,2},{4,5},{5,4},{6,7},{7,6},{8,9},{9,8},{10,11... | collective-permute-start | bytes 25952264 | tf_op jit(solution)/shard_map/ppermute | solution.py:30
  163.6 9.8 %copy-start.22 = (f32[4]{0:T(128)S(1)}, f32[4]{0:T(128)}, u32[]{:S(2)}) copy-start(f32[4]{0:T(128)} %param.17) | copy-start | bytes 52
  170.9 0.8 copy-start.5
  170.9 1.9 copy-start.7
  181.9 3.1 %copy-start.14 = (f32[2,512,4]{1,2,0:T(4,128)S(1)}, f32[2,512,4]{1,2,0:T(4,128)}, u32[]{:S(2)}) copy-start(f32[2,512,4]{1,2,0:T(4,128)} %copy-done.13) | copy-start | bytes 49156
  181.9 3.1 %copy-start.23 = (f32[4]{0:T(128)S(1)}, f32[4]{0:T(128)}, u32[]{:S(2)}) copy-start(f32[4]{0:T(128)} %param.17) | copy-start | bytes 52
  181.9 3.9 %copy-start.11 = (f32[6,512]{1,0:T(8,128)S(1)}, f32[6,512]{1,0:T(8,128)}, u32[]{:S(2)}) copy-start(f32[6,512]{1,0:T(8,128)} %fusion.61) | copy-start | bytes 36868
  185.0 3.3 %copy-start.3 = (f32[6,1024,16]{1,0,2:T(8,128)S(1)}, f32[6,1024,16]{1,0,2:T(8,128)}, u32[]{:S(2)}) copy-start(f32[6,1024,16]{1,0,2:T(8,128)} %fusion.73) | copy-start | bytes 1179652
  185.0 3.3 %copy-start.20 = (s32[1,6]{1,0:T(1,128)S(1)}, s32[1,6]{1,0:T(1,128)}, u32[]{:S(2)}) copy-start(s32[1,6]{1,0:T(1,128)} %param.21) | copy-start | bytes 76
  185.1 3.3 %copy-start.24 = (s32[32]{0:T(128)S(1)}, s32[32]{0:T(128)}, u32[]{:S(2)}) copy-start(s32[32]{0:T(128)} %iota_add_fusion) | copy-start | bytes 388
  185.8 4.2 %copy-start.6 = (bf16[256,1024]{1,0:T(8,128)(2,1)S(1)}, bf16[256,1024]{1,0:T(8,128)(2,1)}, u32[]{:S(2)}) copy-start(bf16[256,1024]{1,0:T(8,128)(2,1)} %copy-done.5) | copy-start | bytes 1572868
  185.8 4.2 %copy-start.8 = (bf16[256,1024]{1,0:T(8,128)(2,1)S(1)}, bf16[256,1024]{1,0:T(8,128)(2,1)}, u32[]{:S(2)}) copy-start(bf16[256,1024]{1,0:T(8,128)(2,1)} %copy-done.7) | copy-start | bytes 1572868
  196.8 2.3 %copy-start.9 = (bf16[1,512,512]{1,2,0:T(8,128)(2,1)S(1)}, bf16[1,512,512]{1,2,0:T(8,128)(2,1)}, u32[]{:S(2)}) copy-start(bf16[1,512,512]{1,2,0:T(8,128)(2,1)} %get-tuple-element.8) | copy-start | bytes 1572868
  196.8 2.4 %copy-start.10 = (bf16[1,512,512]{1,2,0:T(8,128)(2,1)S(1)}, bf16[1,512,512]{1,2,0:T(8,128)(2,1)}, u32[]{:S(2)}) copy-start(bf16[1,512,512]{1,2,0:T(8,128)(2,1)} %get-tuple-element.7) | copy-start | bytes 1572868
  196.8 2.4 %copy-start.16 = (f32[512,4]{0,1:T(4,128)S(1)}, f32[512,4]{0,1:T(4,128)}, u32[]{:S(2)}) copy-start(f32[512,4]{0,1:T(4,128)} %fusion.69) | copy-start | bytes 24580
  196.8 2.4 %copy-start.19 = (f32[1,4,4,128]{3,1,2,0:T(4,128)S(1)}, f32[1,4,4,128]{3,1,2,0:T(4,128)}, u32[]{:S(2)}) copy-start(f32[1,4,4,128]{3,1,2,0:T(4,128)} %copy.86) | copy-start | bytes 24580
  199.2 2.9 %copy-start.18 = (f32[512,4]{0,1:T(4,128)S(1)}, f32[512,4]{0,1:T(4,128)}, u32[]{:S(2)}) copy-start(f32[512,4]{0,1:T(4,128)} %fusion.68) | copy-start | bytes 24580
  202.1 3.1 %copy-start.4 = (bf16[512,1024]{1,0:T(8,128)(2,1)S(1)}, bf16[512,1024]{1,0:T(8,128)(2,1)}, u32[]{:S(2)}) copy-start(bf16[512,1024]{1,0:T(8,128)(2,1)} %param.24) | copy-start | bytes 3145732
  205.2 5.0 %copy-start.2 = (bf16[256,1024]{1,0:T(8,128)(2,1)S(1)}, bf16[256,1024]{1,0:T(8,128)(2,1)}, u32[]{:S(2)}) copy-start(bf16[256,1024]{1,0:T(8,128)(2,1)} %param.13) | copy-start | bytes 1572868
  206.0 5.7 %copy-start.21 = (f32[1,1024]{1,0:T(1,128)S(1)}, f32[1,1024]{1,0:T(1,128)}, u32[]{:S(2)}) copy-start(f32[1,1024]{1,0:T(1,128)} %get-tuple-element.11) | copy-start | bytes 12292
  207.2 3.0 %collective-permute-start.2 = (f32[256,1024]{1,0:T(8,128)}, f32[256,1024]{1,0:T(8,128)}, u32[]{:S(2)}, u32[]{:S(2)}) collective-permute-start(f32[256,1024]{1,0:T(8,128)} %constant_dynamic-slice_fusion), channel_id=1, source_target_pairs={{0,1},{1,0},{2,3},{3,2},{4,5},{5,4},{6,7},{7,6},{8,9},{9,8},{10,11... | collective-permute-start | bytes 3145736 | tf_op jit(solution)/shard_map/ppermute | solution.py:30
  223.3 3.9 %copy-start.1 = (bf16[3,1024,512]{2,1,0:T(8,128)(2,1)S(1)}, bf16[3,1024,512]{2,1,0:T(8,128)(2,1)}, u32[]{:S(2)}) copy-start(bf16[3,1024,512]{2,1,0:T(8,128)(2,1)} %param.15) | copy-start | bytes 9437188
  (1 other events, 0.6 us)
Sparse Core Ops, SparseCore 0:
  154.1 40.6 reduce-scatter.1
